TPU v7x, 256 devices: a whole 4x4x8 slice. The times are simulated.
256 devices in a mesh: dp: 16 (over y_lo, x, core), tensor: 16 (over y_hi, z).
Axes of the slice: x: 4, y: 4 (y_hi: 2, y_lo: 2; y = y_hi * 2 + y_lo), z: 8, core: 2. Of those that a mesh axis runs over, the one named last changes fastest.
Arguments:
- tokens: bfloat16 [12288, 8192], P(('dp', 'tensor')), may hold values from -6 to 6
- q_weight: bfloat16 [8192, 8192], P(None, 'tensor'), may hold values from -0.0625 to 0.0625
- pool_down: bfloat16 [128, 64, 8192], P('dp', None, 'tensor'), may hold values from -0.0625 to 0.0625
- pool_up: bfloat16 [128, 64, 8192], P('dp', None, 'tensor'), may hold values from -0.75 to 0.75
- block_units: int32 [16, 8], replicated, may hold values from 1 to 24, 48 in all within a row
- adapter_ids: int32 [16, 8], replicated, may hold values from 0 to 127, as said below
- location: int32 [128], replicated, may hold values from 0 to 127, as said below
Outputs:
- queries: bfloat16 [12288, 8192], P('dp', 'tensor')
Inputs may be any that keep to these rules, and one draw needn't show every extreme that they name: `adapter_ids`: the 8 adapters of one group lie in pool rows of 8 different dp shards (row location[a] lies on shard location[a] // 8). A permutation: adapter a is held in pool row location[a]. `block_units`: each group's blocks sum to 48; the largest is exactly 24.
All inputs are finite; a program needn't handle non-finite values.
Results may differ from a plain program's by a relative error of at most 0.0029.
Values may be sent and summed in bfloat16 or wider, within the bound.
No kernel may reach another device: no remote copies, remote signals or barrier semaphores. Data moves between devices by JAX's collectives and lax.ppermute only.
A program may use at most 128 MiB of HBM per device.

v0:
```python
import jax
import jax.numpy as jnp
from jax import lax
from jax.sharding import PartitionSpec as P

adapter_scale = 0.5


def tenant_mask(pool_unit_row, group_rows, tenants):
    block_ends = 16 * jnp.cumsum(pool_unit_row)
    positions = jnp.arange(group_rows, dtype=jnp.int32)
    tenant_index = jnp.sum((positions[:, None] >= block_ends[None, :]).astype(jnp.int32), axis=1)
    return tenant_index[:, None] == jnp.arange(tenants, dtype=jnp.int32)[None, :]


def select_rows(one_hot, table):
    picked = jnp.einsum(
        "ks,srd->krd", one_hot.astype(jnp.bfloat16), table, preferred_element_type=jnp.float32
    )
    return picked.astype(jnp.bfloat16)


def on_device(tokens, q_weight, pool_down, pool_up, block_units, adapter_ids, location):
    my_group = lax.axis_index("dp")
    tenants = adapter_ids.shape[1]
    rank_size = pool_down.shape[1]
    local_width = pool_down.shape[2]
    columns = q_weight.shape[1]
    pool_total = location.shape[0]
    id_hits = adapter_ids[:, :, None] == jnp.arange(pool_total, dtype=jnp.int32)[None, None, :]
    slot_ids = jnp.sum(jnp.where(id_hits, location[None, None, :], 0), axis=2)
    my_slots = lax.dynamic_index_in_dim(slot_ids, my_group, 0, keepdims=False)
    whole_down, whole_up = (
        lax.all_gather(pool_down, "dp", axis=0, tiled=True),
        lax.all_gather(pool_up, "dp", axis=0, tiled=True),
    )
    pick_rows = my_slots[:, None] == jnp.arange(pool_total, dtype=jnp.int32)[None, :]
    panels_down = select_rows(pick_rows, whole_down)
    panels_up = select_rows(pick_rows, whole_up)
    down_flat = panels_down.reshape(tenants * rank_size, local_width)
    up_flat = panels_up.reshape(tenants * rank_size, columns)
    width_start = lax.axis_index("tensor") * local_width
    row_block = lax.all_gather(tokens, "tensor", axis=0, tiled=True)
    base_projection = jnp.dot(row_block, q_weight, preferred_element_type=jnp.float32)
    local_cols = lax.dynamic_slice_in_dim(row_block, width_start, local_width, 1)
    wide_part = lax.dot_general(
        local_cols, down_flat, (((1,), (1,)), ((), ())), preferred_element_type=jnp.float32
    )
    combined = jnp.concatenate([base_projection, wide_part], axis=1)
    group_rows = combined.shape[0]
    base_projection = combined[:, :columns]
    wide_part = combined[:, columns:].reshape(group_rows, tenants, rank_size)
    pool_unit_row = lax.dynamic_index_in_dim(block_units, my_group, 0, keepdims=False)
    tenant_masks = tenant_mask(pool_unit_row, group_rows, tenants)
    partial_low = jnp.sum(
        jnp.where(tenant_masks[:, :, None], wide_part, jnp.zeros((), jnp.float32)), axis=1
    )
    packed = partial_low.reshape(group_rows * rank_size // 128, 128)
    low_rank = lax.psum(packed, "tensor").astype(jnp.bfloat16)
    low_rank = low_rank.reshape(group_rows, rank_size)
    low_wide = jnp.where(
        tenant_masks[:, :, None], low_rank[:, None, :], jnp.zeros((), jnp.bfloat16)
    )
    adapter_contribution = jnp.dot(
        low_wide.reshape(group_rows, tenants * rank_size),
        up_flat,
        preferred_element_type=jnp.float32,
    )
    return (base_projection + adapter_scale * adapter_contribution).astype(jnp.bfloat16)


def solution(mesh):
    placed = (
        P(("dp", "tensor"), None),
        P(None, "tensor"),
        P("dp", None, "tensor"),
        P("dp", None, "tensor"),
        P(),
        P(),
        P(),
    )
    return jax.shard_map(
        on_device, mesh=mesh, in_specs=placed, out_specs=P("dp", "tensor"), check_vma=False
    )
```

profile of v0, /device:TPU:2, one launch (start us, length us, event | category | flops | bytes accessed | tf_op | source)
XLA Modules:
  0.0 403.1 jit_solution(1845596998475962294)
XLA Ops:
  6.5 0.0 copy-start
  6.5 0.0 all-gather.6.cloned.1.call-start
  6.5 0.7 all-gather.6.cloned.1.call-update
  7.3 0.0 all-gather.8.cloned.1.call-start
  7.3 0.7 all-gather.8.cloned.1.call-update
  8.0 0.0 all-gather.4.cloned.1.call-start
  8.1 0.7 all-gather.4.cloned.1.call-update
  8.7 0.8 copy.18
  9.5 0.0 copy-done
  9.5 0.2 dynamic-slice_reduce_fusion
  9.7 0.2 reduce-window.8
  9.9 1.1 select_reduce_fusion.1
  11.0 0.1 convert_reduce_fusion
  11.1 55.6 %all-gather.6.cloned.1.call-done = bf16[128,64,512]{2,1,0:T(8,128)(2,1)} async-done(((bf16[8,64,512]{2,1,0:T(8,128)(2,1)}), bf16[128,64,512]{2,1,0:T(8,128)(2,1)}) %all-gather.6.cloned.1.call-update) | async-done | bytes 8388624 | tf_op jit(solution)/shard_map/all_gather | solution.py:34
  66.7 12.2 %fusion.6 = bf16[8,64,512]{2,0,1:T(8,128)(2,1)S(1)} fusion(bf16[128,64,512]{2,1,0:T(8,128)(2,1)} %all-gather.6.cloned.1.call-done, s32[8]{0:T(128)S(1)} %fusion.27), kind=kOutput, calls=%fused_computation.8 | convolution fusion | flops 67372032 | bytes 8912928 | tf_op jit(solution)/shard_map/ks,srd->krd/dot_general | solution.py:17
  78.8 45.2 %all-gather.8.cloned.1.call-done = bf16[128,64,512]{2,1,0:T(8,128)(2,1)} async-done(((bf16[8,64,512]{2,1,0:T(8,128)(2,1)}), bf16[128,64,512]{2,1,0:T(8,128)(2,1)}) %all-gather.8.cloned.1.call-update) | async-done | bytes 8388624 | tf_op jit(solution)/shard_map/all_gather | solution.py:35
  124.0 12.3 %fusion.9 = bf16[8,64,512]{2,0,1:T(8,128)(2,1)S(1)} fusion(bf16[128,64,512]{2,1,0:T(8,128)(2,1)} %all-gather.8.cloned.1.call-done, s32[8]{0:T(128)S(1)} %fusion.27), kind=kOutput, calls=%fused_computation.9 | convolution fusion | flops 67372032 | bytes 8912928 | tf_op jit(solution)/shard_map/ks,srd->krd/dot_general | solution.py:17
  136.4 169.6 %all-gather.4.cloned.1.call-done = bf16[768,8192]{1,0:T(8,128)(2,1)} async-done(((bf16[48,8192]{1,0:T(8,128)(2,1)}), bf16[768,8192]{1,0:T(8,128)(2,1)}) %all-gather.4.cloned.1.call-update) | async-done | bytes 12582928 | tf_op jit(solution)/shard_map/all_gather | solution.py:43
  306.0 1.8 select_reduce_fusion
  307.8 0.2 copy.21
  308.0 0.1 reshape.63
  308.1 74.8 %all-reduce.1 = bf16[384,128]{1,0:T(8,128)(2,1)S(1)} all-reduce(f32[384,128]{1,0:T(8,128)S(1)} %reshape.63), channel_id=1, replica_groups=mesh['dp'=16,'tensor'=16] {'tensor'}, use_global_device_ids=true, to_apply=%region_4.5 | all-reduce | flops 49152 | bytes 294912 | tf_op jit(solution)/shard_map/psum | solution.py:59
  382.9 0.1 broadcast_in_dim.59
  383.0 0.1 copy.22
  383.1 0.6 fusion.13
  383.8 12.8 %fusion.5 = bf16[768,512]{1,0:T(8,128)(2,1)} fusion(f32[768,512,1]{1,0,2:T(8,128)S(1)} %fusion.13, bf16[768,8192]{1,0:T(8,128)(2,1)} %all-gather.4.cloned.1.call-done, bf16[8192,512]{1,0:T(8,128)(2,1)} %param.8), kind=kOutput, calls=%fused_computation.6 | convolution fusion | flops 6443630592 | bytes 23330816 | tf_op jit(solution)/shard_map/dot_general | solution.py:44
  (3 shorter events, 0.0 us)
Async XLA Ops:
  6.5 3.0 copy-start
  6.5 60.1 %all-gather.6.cloned.1.call-start = ((), (), s32[]{:S(2)}) async-start(), calls=%async_computation.1 | async-start | bytes 8912896 | tf_op jit(solution)/shard_map/all_gather | solution.py:34
  7.3 116.8 %all-gather.8.cloned.1.call-start = ((), (), s32[]{:S(2)}) async-start(), calls=%async_computation.2 | async-start | bytes 8912896 | tf_op jit(solution)/shard_map/all_gather | solution.py:35
  8.0 298.0 %all-gather.4.cloned.1.call-start = ((), (), s32[]{:S(2)}) async-start(), calls=%async_computation | async-start | bytes 13369344 | tf_op jit(solution)/shard_map/all_gather | solution.py:43
Sparse Core Ops, SparseCore 0:
  9.2 57.4 all-gather.5
  68.5 55.4 all-gather.7
  126.6 179.3 all-gather.3
where the time goes:
time: 403 us
  waiting for transfers between devices  272 us (67%)
  blocking collectives  74.8 us (19%)
  matrix products  39.7 us (10%)
  between operations  13.2 us (3%)
    all_gather x1, waiting for transfers between devices, on_device(): row_block = lax.all_gather(tokens, 'tensor', axis=0, tiled=True)  170 us
    psum x1, blocking collectives, on_device(): low_rank = lax.psum(packed, 'tensor').astype(jnp.bfloat16)  74.8 us
    all_gather x1, waiting for transfers between devices, on_device(): lax.all_gather(pool_down, 'dp', axis=0, tiled=True)  55.6 us
    all_gather x1, waiting for transfers between devices, on_device(): lax.all_gather(pool_up, 'dp', axis=0, tiled=True)  45.2 us
    dot_general x2, matrix products, select_rows(): jnp.einsum('ks,srd->krd', one_hot.astype(jnp.bfloat16), table, preferred_...  24.5 us
    dot_general x1, matrix products, on_device(): jnp.dot(row_block, q_weight, preferred_element_type=jnp.float32)  12.8 us
  transfers between devices with their start and end apart: 3, of which 3 were waited for; matrix products, arithmetic and copies ran while one was open for 7% of the time, Pallas kernels for 0%

commit v1 on v0

--- a/solution.py
+++ b/solution.py
@@ -40,7 +40,9 @@
     down_flat = panels_down.reshape(tenants * rank_size, local_width)
     up_flat = panels_up.reshape(tenants * rank_size, columns)
     width_start = lax.axis_index("tensor") * local_width
-    row_block = lax.all_gather(tokens, "tensor", axis=0, tiled=True)
+    out_arr = jnp.stack([tokens] * lax.axis_size("tensor"), 0)
+    e_next = lax.all_to_all(out_arr, "tensor", concat_axis=0, split_axis=0)
+    row_block = jnp.concatenate(e_next, 0)
     base_projection = jnp.dot(row_block, q_weight, preferred_element_type=jnp.float32)
     local_cols = lax.dynamic_slice_in_dim(row_block, width_start, local_width, 1)
     wide_part = lax.dot_general(

time: 403 us -> 413 us (1.025)
  waiting for transfers between devices: 272 us -> 255 us
  starting transfers between devices: 0.08 us -> 11.4 us
  blocking collectives: 74.8 us -> 83.4 us
  local copies, waits for them, and re-layouts: 1.49 us -> 7.97 us
    all_gather x1 -> x0, waiting for transfers between devices: 170 us -> none  [on_device(): row_block = lax.all_gather(tokens, 'tensor', axis=0, tiled=True)]
    all_gather x1, waiting for transfers between devices: 45.2 us -> 110 us  [on_device(): lax.all_gather(pool_up, 'dp', axis=0, tiled=True)]
    all_to_all x0 -> x1, waiting for transfers between devices: none -> 54.8 us  [on_device(): e_next = lax.all_to_all(out_arr, 'tensor', concat_axis=0, split_axis=0)]
    all_gather x1, waiting for transfers between devices: 55.6 us -> 88.4 us  [on_device(): lax.all_gather(pool_down, 'dp', axis=0, tiled=True)]
    all_to_all x0 -> x1, starting transfers between devices: none -> 11.4 us  [on_device(): e_next = lax.all_to_all(out_arr, 'tensor', concat_axis=0, split_axis=0)]
    psum x1, blocking collectives: 74.8 us -> 83.4 us  [on_device(): low_rank = lax.psum(packed, 'tensor').astype(jnp.bfloat16)]
    another operation x0 -> x1, local copies, waits for them, and re-layouts: none -> 7.16 us  [on_device(): out_arr = jnp.stack([tokens] * lax.axis_size('tensor'), 0)]
  transfers between devices with their start and end apart: 3 -> 3, of which waited for: 3 -> 3; matrix products, arithmetic and copies ran while one was open for 7% -> 8% of each run, Pallas kernels for 0% -> 0%
where the time goes in v1:
time: 413 us; the launch traced here: 411 us
  waiting for transfers between devices  255 us (62%)
  blocking collectives  83.4 us (20%)
  matrix products  39.7 us (10%)
  between operations  13.5 us (3%)
  starting transfers between devices  11.4 us (3%)
  local copies, waits for them, and re-layouts  7.97 us (2%)
    all_gather x1, waiting for transfers between devices, on_device(): lax.all_gather(pool_up, 'dp', axis=0, tiled=True)  110 us
    all_gather x1, waiting for transfers between devices, on_device(): lax.all_gather(pool_down, 'dp', axis=0, tiled=True)  88.4 us
    psum x1, blocking collectives, on_device(): low_rank = lax.psum(packed, 'tensor').astype(jnp.bfloat16)  83.4 us
    all_to_all x1, waiting for transfers between devices, on_device(): e_next = lax.all_to_all(out_arr, 'tensor', concat_axis=0, split_axis=0)  54.8 us
    dot_general x2, matrix products, select_rows(): jnp.einsum('ks,srd->krd', one_hot.astype(jnp.bfloat16), table, preferred_...  24.5 us
    dot_general x1, matrix products, on_device(): jnp.dot(row_block, q_weight, preferred_element_type=jnp.float32)  12.8 us
    all_to_all x1, starting transfers between devices, on_device(): e_next = lax.all_to_all(out_arr, 'tensor', concat_axis=0, split_axis=0)  11.4 us
  transfers between devices with their start and end apart: 3, of which 3 were waited for; matrix products, arithmetic and copies ran while one was open for 8% of the time, Pallas kernels for 0%

profile of v1, /device:TPU:2, one launch (start us, length us, event | category | flops | bytes accessed | tf_op | source)
XLA Modules:
  0.0 411.5 jit_solution(17513035172935970253)
XLA Ops:
  6.5 0.0 copy-start
  6.5 0.0 all-gather.3.cloned.1.call-start
  6.5 0.7 all-gather.3.cloned.1.call-update
  7.3 7.2 %stack.2 = bf16[16,48,8192]{2,1,0:T(8,128)(2,1)} broadcast(bf16[48,8192]{1,0:T(8,128)(2,1)} %param.7), dimensions={1,2} | broadcast | bytes 13369344 | tf_op jit(solution)/shard_map/stack | solution.py:43
  14.4 0.0 copy-start.1
  14.4 0.0 copy-start.2
  14.4 11.4 %all-to-all-start = ((bf16[16,48,8192]{2,1,0:T(8,128)(2,1)}), bf16[16,48,8192]{2,1,0:T(8,128)(2,1)}, u32[]{:S(2)}, u32[]{:S(2)}) async-start(bf16[16,48,8192]{2,1,0:T(8,128)(2,1)} %stack.2), calls=%async_computation | async-start | bytes 25165824 | tf_op jit(solution)/shard_map/all_to_all | solution.py:44
  25.8 0.0 all-gather.5.cloned.1.call-start
  25.9 0.7 all-gather.5.cloned.1.call-update
  26.6 0.0 copy-done.1
  26.6 0.1 copy.18
  26.6 0.0 copy-done
  26.6 0.2 dynamic-slice_reduce_fusion
  26.8 0.2 reduce-window.8
  27.0 0.0 copy-done.2
  27.0 0.4 select_reduce_fusion.1
  27.5 0.1 convert_reduce_fusion
  27.6 88.4 %all-gather.3.cloned.1.call-done = bf16[128,64,512]{2,1,0:T(8,128)(2,1)} async-done(((bf16[8,64,512]{2,1,0:T(8,128)(2,1)}), bf16[128,64,512]{2,1,0:T(8,128)(2,1)}) %all-gather.3.cloned.1.call-update) | async-done | bytes 8388624 | tf_op jit(solution)/shard_map/all_gather | solution.py:34
  115.9 12.2 %fusion.6 = bf16[8,64,512]{2,0,1:T(8,128)(2,1)S(1)} fusion(bf16[128,64,512]{2,1,0:T(8,128)(2,1)} %all-gather.3.cloned.1.call-done, s32[8]{0:T(128)S(1)} %fusion.27), kind=kOutput, calls=%fused_computation.8 | convolution fusion | flops 67372032 | bytes 8912928 | tf_op jit(solution)/shard_map/ks,srd->krd/dot_general | solution.py:17
  128.1 110.2 %all-gather.5.cloned.1.call-done = bf16[128,64,512]{2,1,0:T(8,128)(2,1)} async-done(((bf16[8,64,512]{2,1,0:T(8,128)(2,1)}), bf16[128,64,512]{2,1,0:T(8,128)(2,1)}) %all-gather.5.cloned.1.call-update) | async-done | bytes 8388624 | tf_op jit(solution)/shard_map/all_gather | solution.py:35
  238.3 12.3 %fusion.9 = bf16[8,64,512]{2,0,1:T(8,128)(2,1)S(1)} fusion(bf16[128,64,512]{2,1,0:T(8,128)(2,1)} %all-gather.5.cloned.1.call-done, s32[8]{0:T(128)S(1)} %fusion.27), kind=kOutput, calls=%fused_computation.9 | convolution fusion | flops 67372032 | bytes 8912928 | tf_op jit(solution)/shard_map/ks,srd->krd/dot_general | solution.py:17
  250.6 54.8 %all-to-all-done = bf16[16,48,8192]{2,1,0:T(8,128)(2,1)} async-done(((bf16[16,48,8192]{2,1,0:T(8,128)(2,1)}), bf16[16,48,8192]{2,1,0:T(8,128)(2,1)}, u32[]{:S(2)}, u32[]{:S(2)}) %all-to-all-start) | async-done | bytes 12582944 | tf_op jit(solution)/shard_map/all_to_all | solution.py:44
  305.4 1.8 select_reduce_fusion
  307.2 0.2 copy.21
  307.4 0.1 reshape.69
  307.5 83.4 %all-reduce.1 = bf16[384,128]{1,0:T(8,128)(2,1)S(1)} all-reduce(f32[384,128]{1,0:T(8,128)S(1)} %reshape.69), channel_id=1, replica_groups=mesh['dp'=16,'tensor'=16] {'tensor'}, use_global_device_ids=true, to_apply=%region_4.5 | all-reduce | flops 49152 | bytes 294912 | tf_op jit(solution)/shard_map/psum | solution.py:61
  390.9 0.1 broadcast_in_dim.59
  391.1 0.1 copy.22
  391.2 0.6 fusion.13
  391.8 12.8 %fusion.5 = bf16[768,512]{1,0:T(8,128)(2,1)} fusion(f32[768,512,1]{1,0,2:T(8,128)S(1)} %fusion.13, bf16[768,8192]{1,0:T(8,128)(2,1)} %bitcast, bf16[8192,512]{1,0:T(8,128)(2,1)} %param.8), kind=kOutput, calls=%fused_computation.6 | convolution fusion | flops 6443630592 | bytes 23330816 | tf_op jit(solution)/shard_map/dot_general | solution.py:46
  (3 shorter events, 0.0 us)
Async XLA Ops:
  6.5 20.1 %copy-start = (s32[16,8]{0,1:T(8,128)S(1)}, s32[16,8]{0,1:T(8,128)}, u32[]{:S(2)}) copy-start(s32[16,8]{0,1:T(8,128)} %param.11) | copy-start | bytes 1540
  6.5 109.4 %all-gather.3.cloned.1.call-start = ((), (), s32[]{:S(2)}) async-start(), calls=%async_computation.1 | async-start | bytes 8912896 | tf_op jit(solution)/shard_map/all_gather | solution.py:34
  14.4 12.1 %copy-start.1 = (s32[16,8]{0,1:T(8,128)S(1)}, s32[16,8]{0,1:T(8,128)}, u32[]{:S(2)}) copy-start(s32[16,8]{0,1:T(8,128)} %param.12) | copy-start | bytes 1540
  14.4 12.6 %copy-start.2 = (s32[128]{0:T(128)S(1)}, s32[128]{0:T(128)}, u32[]{:S(2)}) copy-start(s32[128]{0:T(128)} %param.13) | copy-start | bytes 1540
  14.4 291.0 %all-to-all-start = ((bf16[16,48,8192]{2,1,0:T(8,128)(2,1)}), bf16[16,48,8192]{2,1,0:T(8,128)(2,1)}, u32[]{:S(2)}, u32[]{:S(2)}) async-start(bf16[16,48,8192]{2,1,0:T(8,128)(2,1)} %stack.2), calls=%async_computation | async-start | bytes 25165824 | tf_op jit(solution)/shard_map/all_to_all | solution.py:44
  25.8 212.5 %all-gather.5.cloned.1.call-start = ((), (), s32[]{:S(2)}) async-start(), calls=%async_computation.2 | async-start | bytes 8912896 | tf_op jit(solution)/shard_map/all_gather | solution.py:35
Sparse Core Ops, SparseCore 0:
  9.2 106.6 all-gather.2
  117.8 120.4 all-gather.4

commit v2 on v0

--- a/solution.py
+++ b/solution.py
@@ -56,7 +56,7 @@
         jnp.where(tenant_masks[:, :, None], wide_part, jnp.zeros((), jnp.float32)), axis=1
     )
     packed = partial_low.reshape(group_rows * rank_size // 128, 128)
-    low_rank = lax.psum(packed, "tensor").astype(jnp.bfloat16)
+    low_rank = jnp.sum(jax.lax.all_gather(packed, "tensor"), axis=0).astype(jnp.bfloat16)
     low_rank = low_rank.reshape(group_rows, rank_size)
     low_wide = jnp.where(
         tenant_masks[:, :, None], low_rank[:, None, :], jnp.zeros((), jnp.bfloat16)

time: 403 us -> 420 us (1.042)
  waiting for transfers between devices: 272 us -> 361 us
  blocking collectives: 74.8 us -> 0 us
    all_gather x0 -> x1, waiting for transfers between devices: none -> 83.5 us  [on_device(): jax.lax.all_gather(packed, 'tensor')]
    psum x1 -> x0, blocking collectives: 74.8 us -> none  [on_device(): low_rank = lax.psum(packed, 'tensor').astype(jnp.bfloat16)]
    all_gather x1, waiting for transfers between devices: 45.2 us -> 50.4 us  [on_device(): lax.all_gather(pool_up, 'dp', axis=0, tiled=True)]
  transfers between devices with their start and end apart: 3 -> 4, of which waited for: 3 -> 4; matrix products, arithmetic and copies ran while one was open for 7% -> 7% of each run, Pallas kernels for 0% -> 0%
where the time goes in v2:
time: 420 us
  waiting for transfers between devices  361 us (86%)
  matrix products  39.7 us (9%)
  between operations  13.2 us (3%)
    all_gather x1, waiting for transfers between devices, on_device(): row_block = lax.all_gather(tokens, 'tensor', axis=0, tiled=True)  170 us
    all_gather x1, waiting for transfers between devices, on_device(): jax.lax.all_gather(packed, 'tensor')  83.5 us
    all_gather x1, waiting for transfers between devices, on_device(): lax.all_gather(pool_down, 'dp', axis=0, tiled=True)  55.5 us
    all_gather x1, waiting for transfers between devices, on_device(): lax.all_gather(pool_up, 'dp', axis=0, tiled=True)  50.4 us
    dot_general x2, matrix products, select_rows(): jnp.einsum('ks,srd->krd', one_hot.astype(jnp.bfloat16), table, preferred_...  24.5 us
    dot_general x1, matrix products, on_device(): jnp.dot(row_block, q_weight, preferred_element_type=jnp.float32)  12.8 us
  transfers between devices with their start and end apart: 4, of which 4 were waited for; matrix products, arithmetic and copies ran while one was open for 7% of the time, Pallas kernels for 0%

profile of v2, /device:TPU:2, one launch (start us, length us, event | category | flops | bytes accessed | tf_op | source)
XLA Modules:
  0.0 419.9 jit_solution(1842811214956417207)
XLA Ops:
  6.5 0.0 copy-start
  6.5 0.0 all-gather.7.cloned.1.call-start
  6.5 0.7 all-gather.7.cloned.1.call-update
  7.3 0.0 all-gather.5.cloned.1.call-start
  7.3 0.7 all-gather.5.cloned.1.call-update
  8.0 0.0 all-gather.11.cloned.1.call-start
  8.1 0.7 all-gather.11.cloned.1.call-update
  8.7 0.0 all-gather.9.cloned.1.call-start
  8.8 0.8 copy.18
  9.6 0.0 copy-done
  9.6 0.2 dynamic-slice_reduce_fusion
  9.7 0.2 reduce-window.8
  9.9 1.1 select_reduce_fusion.1
  11.0 0.1 convert_reduce_fusion
  11.1 55.5 %all-gather.7.cloned.1.call-done = bf16[128,64,512]{2,1,0:T(8,128)(2,1)} async-done(((bf16[8,64,512]{2,1,0:T(8,128)(2,1)}), bf16[128,64,512]{2,1,0:T(8,128)(2,1)}) %all-gather.7.cloned.1.call-update) | async-done | bytes 8388624 | tf_op jit(solution)/shard_map/all_gather | solution.py:34
  66.7 12.2 %fusion.6 = bf16[8,64,512]{2,0,1:T(8,128)(2,1)S(1)} fusion(bf16[128,64,512]{2,1,0:T(8,128)(2,1)} %all-gather.7.cloned.1.call-done, s32[8]{0:T(128)S(1)} %fusion.27), kind=kOutput, calls=%fused_computation.8 | convolution fusion | flops 67372032 | bytes 8912928 | tf_op jit(solution)/shard_map/ks,srd->krd/dot_general | solution.py:17
  78.8 169.8 %all-gather.5.cloned.1.call-done = bf16[768,8192]{1,0:T(8,128)(2,1)} async-done(((bf16[48,8192]{1,0:T(8,128)(2,1)}), bf16[768,8192]{1,0:T(8,128)(2,1)}) %all-gather.5.cloned.1.call-update) | async-done | bytes 12582928 | tf_op jit(solution)/shard_map/all_gather | solution.py:43
  248.6 1.8 select_reduce_fusion
  250.4 0.2 copy.21
  250.6 0.8 all_gather_reshape.3
  251.4 0.0 all-gather.9.cloned.1.call-update
  251.4 50.4 %all-gather.11.cloned.1.call-done = bf16[128,64,512]{2,1,0:T(8,128)(2,1)} async-done(((bf16[8,64,512]{2,1,0:T(8,128)(2,1)}), bf16[128,64,512]{2,1,0:T(8,128)(2,1)}) %all-gather.11.cloned.1.call-update) | async-done | bytes 8388624 | tf_op jit(solution)/shard_map/all_gather | solution.py:35
  301.8 12.3 %fusion.9 = bf16[8,64,512]{2,0,1:T(8,128)(2,1)S(1)} fusion(bf16[128,64,512]{2,1,0:T(8,128)(2,1)} %all-gather.11.cloned.1.call-done, s32[8]{0:T(128)S(1)} %fusion.27), kind=kOutput, calls=%fused_computation.9 | convolution fusion | flops 67372032 | bytes 8912928 | tf_op jit(solution)/shard_map/ks,srd->krd/dot_general | solution.py:17
  314.1 83.5 %all-gather.9.cloned.1.call-done = f32[16,384,128]{2,1,0:T(8,128)} async-done(((f32[1,384,128]{2,1,0:T(8,128)}), f32[16,384,128]{2,1,0:T(8,128)}) %all-gather.9.cloned.1.call-update) | async-done | bytes 3145744 | tf_op jit(solution)/shard_map/all_gather | solution.py:59
  397.7 2.0 reduce_sum.39
  399.7 0.1 convert_element_type.27
  399.8 0.1 copy.22
  400.0 0.6 fusion.13
  400.6 12.8 %fusion.5 = bf16[768,512]{1,0:T(8,128)(2,1)} fusion(f32[768,512,1]{1,0,2:T(8,128)S(1)} %fusion.13, bf16[768,8192]{1,0:T(8,128)(2,1)} %all-gather.5.cloned.1.call-done, bf16[8192,512]{1,0:T(8,128)(2,1)} %param.8), kind=kOutput, calls=%fused_computation.6 | convolution fusion | flops 6443630592 | bytes 23330816 | tf_op jit(solution)/shard_map/dot_general | solution.py:44
  (3 shorter events, 0.0 us)
Async XLA Ops:
  6.5 3.0 copy-start
  6.5 60.1 %all-gather.7.cloned.1.call-start = ((), (), s32[]{:S(2)}) async-start(), calls=%async_computation.1 | async-start | bytes 8912896 | tf_op jit(solution)/shard_map/all_gather | solution.py:34
  7.3 241.4 %all-gather.5.cloned.1.call-start = ((), (), s32[]{:S(2)}) async-start(), calls=%async_computation | async-start | bytes 13369344 | tf_op jit(solution)/shard_map/all_gather | solution.py:43
  8.0 293.8 %all-gather.11.cloned.1.call-start = ((), (), s32[]{:S(2)}) async-start(), calls=%async_computation.3 | async-start | bytes 8912896 | tf_op jit(solution)/shard_map/all_gather | solution.py:35
  8.7 388.9 %all-gather.9.cloned.1.call-start = ((), (), s32[]{:S(2)}) async-start(), calls=%async_computation.2 | async-start | bytes 3342336 | tf_op jit(solution)/shard_map/all_gather | solution.py:59
Sparse Core Ops, SparseCore 0:
  9.2 57.4 all-gather.6
  69.2 179.3 all-gather.4
  250.5 51.2 all-gather.10
  304.2 93.3 all-gather.8
